TPU v7x, 32 devices: a whole 2x2x4 slice. The times are simulated.
32 devices in a mesh: row: 4 (over x, core), col: 8 (over z, y).
Axes of the slice: x: 2, y: 2, z: 4, core: 2. Of those that a mesh axis runs over, the one named last changes fastest.
Arguments:
- embed: bfloat16 [1024, 768], P(('row', 'col'))
- beta: bfloat16 [1024], P(('row', 'col')), may hold values from 16 to 400
- block_mask: int32 [8, 8], P('row'), may hold values from 0 to 1, as said below
- counts: int32 [8], replicated, may hold values from 2 to 128
- probes: float32 [64, 1024], P(None, ('row', 'col')), may hold values from -6 to 6
Outputs:
- spectral: float32 [64, 1024], P(None, ('row', 'col'))
Inputs may be any that keep to these rules, and one draw needn't show every extreme that they name: `block_mask`: every diagonal entry is 1.
All inputs are finite; a program needn't handle non-finite values.
Results may differ from a plain program's by a relative error of at most 0.012.
The roundings to bfloat16 on the way count: a program that leaves them out, or rounds other values in their place, can miss the bound.
Values may be sent and summed in bfloat16 or wider, within the bound.
No kernel may reach another device: no remote copies, remote signals or barrier semaphores. Data moves between devices by JAX's collectives and lax.ppermute only.
A program may use at most 64 MiB of HBM per device.

v0:
```python
import jax
import jax.numpy as jnp
from jax import lax
from jax.sharding import PartitionSpec as P

ITERS = 2


def spread(shard, axis, root):
    mine = lax.axis_index(axis) == root
    return lax.psum(jnp.where(mine, shard, jnp.zeros_like(shard)), axis)


def own_piece(totals, col_ratio, n_row, row_index, col_index):
    shard_len = totals.shape[1] // n_row
    chosen = jnp.zeros_like(totals)
    for root_k in range(col_ratio):
        received = spread(totals, "col", col_ratio * row_index + root_k)
        chosen = jnp.where(col_index // n_row == root_k, received, chosen)
    return lax.dynamic_slice_in_dim(chosen, col_index % n_row * shard_len, shard_len, 1)


def body(embed, beta, block_mask, counts, probes):
    n_row = lax.axis_size("row")
    n_col = lax.axis_size("col")
    col_ratio = n_col // n_row
    row_index = lax.axis_index("row")
    col_index = lax.axis_index("col")
    shard_len, feat_width = embed.shape
    row_files = shard_len * n_col
    col_files = shard_len * n_row
    values = embed.astype(jnp.float32)
    unit_vec = (
        values * lax.rsqrt(jnp.mean(values * values, axis=1, keepdims=True) + 1e-06)
    ).astype(jnp.bfloat16)
    unit_rows, beta_rows = (
        lax.all_gather(unit_vec, "col", axis=0, tiled=True),
        lax.all_gather(beta, "col", axis=0, tiled=True),
    )
    half_pick = col_index % col_ratio
    col_seq = lax.iota(jnp.int32, col_files)
    unit_cols = spread(
        lax.dynamic_slice_in_dim(unit_rows, half_pick * col_files, col_files, 0),
        "row",
        col_index // col_ratio,
    )
    col_ids = col_index * col_files + col_seq
    gram_tile = lax.dot_general(
        unit_rows, unit_cols, (((1,), (1,)), ((), ())), preferred_element_type=jnp.float32
    )
    scores = gram_tile * (beta_rows.astype(jnp.float32) / feat_width)[:, None]
    row_blocks = block_mask.shape[0]
    blk_size = row_files // row_blocks
    col_block = col_ids // blk_size
    col_live = col_ids % blk_size < jnp.take(counts, col_block, axis=0)
    mask_cols = jnp.take(block_mask, col_block, axis=1) == 1
    block_wide = jnp.broadcast_to(mask_cols[:, None, :], (row_blocks, blk_size, col_files)).reshape(
        row_files, col_files
    )
    row_ids = row_index * row_files + lax.iota(jnp.int32, row_files)
    allowed = block_wide & col_live[None, :] & (row_ids[:, None] != col_ids[None, :])
    masked = jnp.where(allowed, scores, -1e30)
    local_top = jnp.max(masked, axis=1)
    row_top = lax.pmax(local_top, "col")
    row_mass = lax.psum(
        jnp.sum(jnp.where(allowed, jnp.exp(masked - row_top[:, None]), 0.0), axis=1), "col"
    )
    weights = jnp.where(allowed, jnp.exp(masked - row_top[:, None]) / row_mass[:, None], 0.0)
    col_mass = lax.psum(jnp.sum(weights, axis=0), "row")
    own_mass = own_piece(col_mass[None, :], col_ratio, n_row, row_index, col_index)[0]
    inv_root = lax.rsqrt((1.0 + own_mass) * 0.5)
    affinity = weights.astype(jnp.bfloat16)
    probe_state = probes
    for sweep in range(ITERS):
        scaled = (probe_state * inv_root[None, :]).astype(jnp.bfloat16)
        probe_rows = lax.all_gather(scaled, "col", axis=1, tiled=True)
        probe_cols = spread(
            lax.dynamic_slice_in_dim(probe_rows, half_pick * col_files, col_files, 1),
            "row",
            col_index // col_ratio,
        )
        row_part = lax.dot_general(
            probe_cols, affinity, (((1,), (1,)), ((), ())), preferred_element_type=jnp.float32
        )
        col_part = jnp.dot(probe_rows, affinity, preferred_element_type=jnp.float32)
        own_rows = lax.psum_scatter(
            row_part.astype(jnp.bfloat16), "col", scatter_dimension=1, tiled=True
        ).astype(jnp.float32)
        col_total = lax.psum(col_part, "row")
        own_cols = own_piece(col_total, col_ratio, n_row, row_index, col_index)
        probe_state = (own_rows + own_cols) * (0.5 * inv_root)[None, :]
    return probe_state


def solution(mesh):
    placed = (
        P(("row", "col"), None),
        P(("row", "col")),
        P("row", None),
        P(),
        P(None, ("row", "col")),
    )
    return jax.shard_map(
        body, mesh=mesh, in_specs=placed, out_specs=P(None, ("row", "col")), check_vma=False
    )
```

profile of v0, /device:TPU:0, one launch (start us, length us, event | category | flops | bytes accessed | tf_op | source)
XLA Modules:
  0.0 495.1 jit_solution(6957773946014642195)
XLA Ops:
  6.5 0.8 copy-done
  7.5 32.7 %all_gather.12 = bf16[256,768]{1,0:T(8,128)(2,1)S(1)} all-gather(bf16[32,768]{1,0:T(8,128)(2,1)S(1)} %fusion.2), channel_id=1, replica_groups=mesh['row'=4,'col'=8] {'col'}, dimensions={0}, use_global_device_ids=true | all-gather | bytes 442368 | tf_op jit(solution)/shard_map/all_gather | solution.py:37
  40.3 0.7 dynamic-slice_select_fusion
  41.2 0.6 copy-done.1
  41.8 0.7 fusion.21
  42.5 0.7 copy-done.3
  43.3 0.6 gather_fusion
  44.3 0.6 copy-done.5
  46.2 0.6 copy-done.4
  47.0 21.5 %all-reduce = bf16[256]{0:T(256)(128)(2,1)S(1)} all-reduce(bf16[256]{0:T(256)(128)(2,1)S(1)} %dynamic-update-slice), channel_id=1, replica_groups=mesh['row'=4,'col'=8] {'col'}, use_global_device_ids=true, to_apply=%add | all-reduce | flops 256 | bytes 1024
  68.5 5.1 %fusion.12 = pred[128]{0:T(512)(128)(4,1)S(1)} fusion(s32[]{:T(128)} %bitcast.3, s32[]{:T(128)} %bitcast.4, s32[]{:T(128)} %bitcast.5, s32[]{:T(128)} %bitcast.6, s32[]{:T(128)} %bitcast.7, s32[]{:T(128)} %bitcast.8, s32[]{:T(128)} %bitcast.9, s32[]{:T(128)} %bitcast.10, s32[]{:T(128)S(6)} %mul.86), kind=kLoop, calls=%fused_computation.62 | loop fusion | flops 7808 | bytes 164 | tf_op jit(solution)/shard_map/lt | solution.py:55
  74.0 1.2 fusion.22
  75.2 21.3 %pmax.7 = f32[256]{0:T(256)S(1)} all-reduce(f32[256]{0:T(256)S(1)} %get-tuple-element.29), channel_id=1, replica_groups=mesh['row'=4,'col'=8] {'col'}, use_global_device_ids=true, to_apply=%region_3.4 | all-reduce | flops 256 | bytes 2048 | tf_op jit(solution)/shard_map/pmax | solution.py:64
  96.7 17.1 %psum.92 = f32[256]{0:T(256)S(1)} all-reduce(f32[256]{0:T(256)S(1)} %select_reduce_fusion), channel_id=1, replica_groups=mesh['row'=4,'col'=8] {'col'}, use_global_device_ids=true, to_apply=%region_5.6 | all-reduce | flops 256 | bytes 2048 | tf_op jit(solution)/shard_map/psum | solution.py:65
  114.0 5.9 %psum.93 = f32[128]{0:T(128)S(1)} all-reduce(f32[128]{0:T(128)S(1)} %get-tuple-element.13), channel_id=1, replica_groups=mesh['row'=4,'col'=8] {'row'}, use_global_device_ids=true, to_apply=%region_7.8 | all-reduce | flops 128 | bytes 1024 | tf_op jit(solution)/shard_map/psum | solution.py:69
  119.9 19.1 %all-reduce.3 = (f32[1,128]{1,0:T(1,128)S(1)}, f32[1,128]{1,0:T(1,128)S(1)}) all-reduce(f32[1,128]{1,0:T(1,128)S(1)} %get-tuple-element.20, f32[1,128]{1,0:T(1,128)S(1)} %get-tuple-element.19), channel_id=1, replica_groups=mesh['row'=4,'col'=8] {'col'}, use_global_device_ids=true, to_apply=%region_8.9 | all-reduce | flops 256 | bytes 2048 | tf_op jit(solution)/shard_map/psum | solution.py:11
  139.2 30.5 %all_gather.14 = bf16[64,256]{0,1:T(8,128)(2,1)S(1)} all-gather(bf16[64,32]{0,1:T(8,128)(2,1)S(1)} %multiply_convert_fusion), channel_id=1, replica_groups=mesh['row'=4,'col'=8] {'col'}, dimensions={1}, use_global_device_ids=true | all-gather | bytes 36864 | tf_op jit(solution)/shard_map/all_gather | solution.py:76
  169.7 10.3 %psum.96 = bf16[64,128]{0,1:T(8,128)(2,1)S(1)} all-reduce(bf16[64,128]{0,1:T(8,128)(2,1)S(1)} %dynamic-slice_select_fusion.2), channel_id=1, replica_groups=mesh['row'=4,'col'=8] {'row'}, use_global_device_ids=true, to_apply=%region_10.11 | all-reduce | flops 8192 | bytes 32768 | tf_op jit(solution)/shard_map/psum | solution.py:11
  180.1 0.8 convolution_convert_fusion.1
  181.0 10.7 %psum.97 = f32[64,128]{0,1:T(8,128)S(1)} all-reduce(f32[64,128]{0,1:T(8,128)S(1)} %fusion.23), channel_id=1, replica_groups=mesh['row'=4,'col'=8] {'row'}, use_global_device_ids=true, to_apply=%region_12.13 | all-reduce | flops 8192 | bytes 65536 | tf_op jit(solution)/shard_map/psum | solution.py:89
  191.8 0.7 broadcast_select_fusion.2
  192.5 46.2 %reduce-scatter.3.cloned.1.call-done = bf16[64,32]{0,1:T(8,128)(2,1)} async-done(((bf16[64,256]{0,1:T(8,128)(2,1)}), bf16[64,32]{0,1:T(8,128)(2,1)}) %reduce-scatter.3.cloned.1.call-update) | async-done | bytes 4112 | tf_op jit(solution)/shard_map/reduce_scatter | solution.py:86
  238.7 72.8 %all-reduce.12.cloned.1.call-done = (f32[64,128]{0,1:T(8,128)}, f32[64,128]{0,1:T(8,128)}) async-done(((f32[64,128]{0,1:T(8,128)}, f32[64,128]{0,1:T(8,128)}), (f32[64,128]{0,1:T(8,128)}, f32[64,128]{0,1:T(8,128)})) %all-reduce.12.cloned.1.call-update) | async-done | bytes 65552 | tf_op jit(solution)/shard_map/psum | solution.py:11
  311.5 0.8 fusion.9
  312.3 30.5 %all_gather.15 = bf16[64,256]{0,1:T(8,128)(2,1)S(1)} all-gather(bf16[64,32]{0,1:T(8,128)(2,1)S(1)} %fusion.9), channel_id=1, replica_groups=mesh['row'=4,'col'=8] {'col'}, dimensions={1}, use_global_device_ids=true | all-gather | bytes 36864 | tf_op jit(solution)/shard_map/all_gather | solution.py:76
  343.0 10.3 %psum.100 = bf16[64,128]{0,1:T(8,128)(2,1)S(1)} all-reduce(bf16[64,128]{0,1:T(8,128)(2,1)S(1)} %dynamic-slice_select_fusion.1), channel_id=1, replica_groups=mesh['row'=4,'col'=8] {'row'}, use_global_device_ids=true, to_apply=%region_15.16 | all-reduce | flops 8192 | bytes 32768 | tf_op jit(solution)/shard_map/psum | solution.py:11
  353.3 0.8 convolution_convert_fusion
  354.2 11.8 %psum.101 = f32[64,128]{0,1:T(8,128)S(1)} all-reduce(f32[64,128]{0,1:T(8,128)S(1)} %fusion.24), channel_id=1, replica_groups=mesh['row'=4,'col'=8] {'row'}, use_global_device_ids=true, to_apply=%region_17.18 | all-reduce | flops 8192 | bytes 65536 | tf_op jit(solution)/shard_map/psum | solution.py:89
  366.0 0.7 broadcast_select_fusion.1
  366.7 48.3 %reduce-scatter.5.cloned.1.call-done = bf16[64,32]{0,1:T(8,128)(2,1)} async-done(((bf16[64,256]{0,1:T(8,128)(2,1)}), bf16[64,32]{0,1:T(8,128)(2,1)}) %reduce-scatter.5.cloned.1.call-update) | async-done | bytes 4112 | tf_op jit(solution)/shard_map/reduce_scatter | solution.py:86
  415.0 72.3 %all-reduce.10.cloned.1.call-done = (f32[64,128]{0,1:T(8,128)}, f32[64,128]{0,1:T(8,128)}) async-done(((f32[64,128]{0,1:T(8,128)}, f32[64,128]{0,1:T(8,128)}), (f32[64,128]{0,1:T(8,128)}, f32[64,128]{0,1:T(8,128)})) %all-reduce.10.cloned.1.call-update) | async-done | bytes 65552 | tf_op jit(solution)/shard_map/psum | solution.py:11
  487.2 1.4 fusion.5
  (45 shorter events, 2.8 us)
Async XLA Ops:
  6.5 0.8 copy-start
  6.5 67.5 %all-reduce.8.cloned.1.call-start = ((), (), s32[]{:S(2)}) async-start(), calls=%async_computation.2 | async-start | bytes 393216 | tf_op jit(solution)/shard_map/psum | solution.py:11
  41.0 197.7 %reduce-scatter.3.cloned.1.call-start = ((), (), s32[]{:S(2)}) async-start(), calls=%async_computation.3 | async-start | bytes 73728 | tf_op jit(solution)/shard_map/reduce_scatter | solution.py:86
  41.2 0.7 copy-start.1
  42.5 0.7 copy-start.3
  44.2 0.7 copy-start.5
  46.1 0.7 copy-start.4
  114.0 25.1 %copy-start.2 = (f32[64,32]{0,1:T(8,128)S(1)}, f32[64,32]{0,1:T(8,128)}, u32[]{:S(2)}) copy-start(f32[64,32]{0,1:T(8,128)} %param.9) | copy-start | bytes 24580
  181.0 130.5 %all-reduce.12.cloned.1.call-start = ((), (), s32[]{:S(2)}) async-start(), calls=%async_computation.6 | async-start | bytes 262144 | tf_op jit(solution)/shard_map/psum | solution.py:11
  192.4 222.5 %reduce-scatter.5.cloned.1.call-start = ((), (), s32[]{:S(2)}) async-start(), calls=%async_computation.4 | async-start | bytes 73728 | tf_op jit(solution)/shard_map/reduce_scatter | solution.py:86
  354.1 133.1 %all-reduce.10.cloned.1.call-start = ((), (), s32[]{:S(2)}) async-start(), calls=%async_computation.5 | async-start | bytes 262144 | tf_op jit(solution)/shard_map/psum | solution.py:11
Sparse Core Ops, SparseCore 0:
  41.1 32.8 all-reduce.7
  181.1 57.5 reduce-scatter.2
  242.6 68.8 all-reduce.11
  354.3 60.6 reduce-scatter.4
  418.3 68.8 all-reduce.9
where the time goes:
time: 496 us; the launch traced here: 495 us
  waiting for transfers between devices  240 us (48%)
  blocking collectives  222 us (45%)
  between operations  14 us (3%)
  other arithmetic  10.2 us (2%)
  local copies, waits for them, and re-layouts  5.8 us (1%)
    psum x3, waiting for transfers between devices, spread(): return lax.psum(jnp.where(mine, shard, jnp.zeros_like(shard)), axis)  145 us
    reduce_scatter x2, waiting for transfers between devices, body(): lax.psum_scatter(row_part.astype(jnp.bfloat16), 'col', scatter_dimension=...  94.5 us
    all_gather x2, blocking collectives, body(): probe_rows = lax.all_gather(scaled, 'col', axis=1, tiled=True)  61 us
    psum x3, blocking collectives, spread(): return lax.psum(jnp.where(mine, shard, jnp.zeros_like(shard)), axis)  39.7 us
    all_gather x1, blocking collectives, body(): lax.all_gather(unit_vec, 'col', axis=0, tiled=True)  32.7 us
    psum x2, blocking collectives, body(): col_total = lax.psum(col_part, 'row')  22.5 us
    unnamed x1, blocking collectives  21.5 us
    pmax x1, blocking collectives, body(): row_top = lax.pmax(local_top, 'col')  21.3 us
  transfers between devices with their start and end apart: 5, of which 5 were waited for; matrix products, arithmetic and copies ran while one was open for 2% of the time, Pallas kernels for 0%

commit v1 on v0

--- a/solution.py
+++ b/solution.py
@@ -73,7 +73,26 @@
     probe_state = probes
     for sweep in range(ITERS):
         scaled = (probe_state * inv_root[None, :]).astype(jnp.bfloat16)
-        probe_rows = lax.all_gather(scaled, "col", axis=1, tiled=True)
+        item_now = lax.axis_size("col")
+        work_now, f_now, main = (item_now, lax.axis_index("col"), scaled.shape[1])
+        parts_seen = [(j, (j + 1) % work_now) for j in range(work_now)]
+        frames = [(j, (j - 1) % work_now) for j in range(work_now)]
+        probe_rows = jnp.zeros(
+            (*scaled.shape[:1], work_now * main, *scaled.shape[2:]), scaled.dtype
+        )
+        moved = w_next = scaled
+        probe_rows = lax.dynamic_update_slice_in_dim(probe_rows, scaled, f_now * main, axis=1)
+        y1 = work_now // 2
+        for m in range(1, y1 + 1):
+            moved = lax.ppermute(moved, perm=parts_seen, axis_name="col")
+            probe_rows = lax.dynamic_update_slice_in_dim(
+                probe_rows, moved, (f_now - m) % work_now * main, axis=1
+            )
+            if m < work_now - y1:
+                w_next = lax.ppermute(w_next, axis_name="col", perm=frames)
+                probe_rows = lax.dynamic_update_slice_in_dim(
+                    probe_rows, w_next, (f_now + m) % work_now * main, axis=1
+                )
         probe_cols = spread(
             lax.dynamic_slice_in_dim(probe_rows, half_pick * col_files, col_files, 1),
             "row",

time: 496 us -> 485 us (0.978)
  blocking collectives: 222 us -> 160 us
  starting transfers between devices: 0.17 us -> 28.6 us
  waiting for transfers between devices: 240 us -> 260 us
    all_gather x2 -> x0, blocking collectives: 61 us -> none  [body(): probe_rows = lax.all_gather(scaled, 'col', axis=1, tiled=True)]
    ppermute x0 -> x14, starting transfers between devices: none -> 28.4 us  [the longest x6 27.5 us: body(): w_next = lax.ppermute(w_next, axis_name='col', perm=frames)]
    ppermute x0 -> x14, waiting for transfers between devices: none -> 22.4 us  [the longest x8 22.4 us: body(): moved = lax.ppermute(moved, perm=parts_seen, axis_name='col')]
  transfers between devices with their start and end apart: 5 -> 19, of which waited for: 5 -> 13; matrix products, arithmetic and copies ran while one was open for 2% -> 2% of each run, Pallas kernels for 0% -> 0%
where the time goes in v1:
time: 485 us; the launch traced here: 484 us
  waiting for transfers between devices  260 us (54%)
  blocking collectives  160 us (33%)
  starting transfers between devices  28.6 us (6%)
  between operations  14.1 us (3%)
  other arithmetic  10.2 us (2%)
  local copies, waits for them, and re-layouts  7.31 us (2%)
    psum x3, waiting for transfers between devices, spread(): return lax.psum(jnp.where(mine, shard, jnp.zeros_like(shard)), axis)  145 us
    reduce_scatter x2, waiting for transfers between devices, body(): lax.psum_scatter(row_part.astype(jnp.bfloat16), 'col', scatter_dimension=...  92.6 us
    psum x3, blocking collectives, spread(): return lax.psum(jnp.where(mine, shard, jnp.zeros_like(shard)), axis)  39.7 us
    all_gather x1, blocking collectives, body(): lax.all_gather(unit_vec, 'col', axis=0, tiled=True)  32.7 us
    ppermute x6, starting transfers between devices, body(): w_next = lax.ppermute(w_next, axis_name='col', perm=frames)  27.5 us
    ppermute x8, waiting for transfers between devices, body(): moved = lax.ppermute(moved, perm=parts_seen, axis_name='col')  22.4 us
    psum x2, blocking collectives, body(): col_total = lax.psum(col_part, 'row')  22.1 us
    unnamed x1, blocking collectives  21.5 us
  transfers between devices with their start and end apart: 19, of which 13 were waited for; matrix products, arithmetic and copies ran while one was open for 2% of the time, Pallas kernels for 0%

profile of v1, /device:TPU:0, one launch (start us, length us, event | category | flops | bytes accessed | tf_op | source)
XLA Modules:
  0.0 484.2 jit_solution(14853227262513990994)
XLA Ops:
  7.5 32.7 %all_gather.6 = bf16[256,768]{1,0:T(8,128)(2,1)S(1)} all-gather(bf16[32,768]{1,0:T(8,128)(2,1)S(1)} %fusion.2), channel_id=1, replica_groups=mesh['row'=4,'col'=8] {'col'}, dimensions={0}, use_global_device_ids=true | all-gather | bytes 442368 | tf_op jit(solution)/shard_map/all_gather | solution.py:37
  47.0 21.5 %all-reduce = bf16[256]{0:T(256)(128)(2,1)S(1)} all-reduce(bf16[256]{0:T(256)(128)(2,1)S(1)} %dynamic-update-slice), channel_id=1, replica_groups=mesh['row'=4,'col'=8] {'col'}, use_global_device_ids=true, to_apply=%add | all-reduce | flops 256 | bytes 1024
  68.5 5.1 %fusion.12 = pred[128]{0:T(512)(128)(4,1)S(1)} fusion(s32[]{:T(128)} %bitcast.3, s32[]{:T(128)} %bitcast.4, s32[]{:T(128)} %bitcast.5, s32[]{:T(128)} %bitcast.6, s32[]{:T(128)} %bitcast.7, s32[]{:T(128)} %bitcast.8, s32[]{:T(128)} %bitcast.9, s32[]{:T(128)} %bitcast.10, s32[]{:T(128)S(6)} %mul.118), kind=kLoop, calls=%fused_computation.78 | loop fusion | flops 7808 | bytes 164 | tf_op jit(solution)/shard_map/lt | solution.py:55
  74.0 1.2 fusion.23
  75.2 21.4 %pmax.7 = f32[256]{0:T(256)S(1)} all-reduce(f32[256]{0:T(256)S(1)} %get-tuple-element.33), channel_id=1, replica_groups=mesh['row'=4,'col'=8] {'col'}, use_global_device_ids=true, to_apply=%region_3.4 | all-reduce | flops 256 | bytes 2048 | tf_op jit(solution)/shard_map/pmax | solution.py:64
  96.7 17.1 %psum.92 = f32[256]{0:T(256)S(1)} all-reduce(f32[256]{0:T(256)S(1)} %select_reduce_fusion), channel_id=1, replica_groups=mesh['row'=4,'col'=8] {'col'}, use_global_device_ids=true, to_apply=%region_5.6 | all-reduce | flops 256 | bytes 2048 | tf_op jit(solution)/shard_map/psum | solution.py:65
  114.0 5.9 %psum.93 = f32[128]{0:T(128)S(1)} all-reduce(f32[128]{0:T(128)S(1)} %get-tuple-element.17), channel_id=1, replica_groups=mesh['row'=4,'col'=8] {'row'}, use_global_device_ids=true, to_apply=%region_7.8 | all-reduce | flops 128 | bytes 1024 | tf_op jit(solution)/shard_map/psum | solution.py:69
  119.9 19.1 %all-reduce.3 = (f32[1,128]{1,0:T(1,128)S(1)}, f32[1,128]{1,0:T(1,128)S(1)}) all-reduce(f32[1,128]{1,0:T(1,128)S(1)} %get-tuple-element.24, f32[1,128]{1,0:T(1,128)S(1)} %get-tuple-element.23), channel_id=1, replica_groups=mesh['row'=4,'col'=8] {'col'}, use_global_device_ids=true, to_apply=%region_8.9 | all-reduce | flops 256 | bytes 2048 | tf_op jit(solution)/shard_map/psum | solution.py:11
  139.9 4.7 collective-permute-start.1
  144.6 1.6 collective-permute-done
  146.3 4.7 collective-permute-start.3
  151.0 1.6 collective-permute-done.2
  152.6 4.7 collective-permute-start.5
  157.3 1.6 collective-permute-done.4
  159.0 6.3 %collective-permute-done.6 = bf16[64,32]{0,1:T(8,128)(2,1)S(1)} collective-permute-done((bf16[64,32]{0,1:T(8,128)(2,1)S(1)}, bf16[64,32]{0,1:T(8,128)(2,1)S(1)}, u32[]{:S(2)}, u32[]{:S(2)}) %collective-permute-start.6) | collective-permute-done | bytes 4128 | tf_op jit(solution)/shard_map/ppermute | solution.py:87
  165.3 10.3 %psum.96 = bf16[64,128]{0,1:T(8,128)(2,1)S(1)} all-reduce(bf16[64,128]{0,1:T(8,128)(2,1)S(1)} %dynamic-slice_select_fusion.2), channel_id=1, replica_groups=mesh['row'=4,'col'=8] {'row'}, use_global_device_ids=true, to_apply=%region_10.11 | all-reduce | flops 8192 | bytes 32768 | tf_op jit(solution)/shard_map/psum | solution.py:11
  176.7 10.7 %psum.97 = f32[64,128]{0,1:T(8,128)S(1)} all-reduce(f32[64,128]{0,1:T(8,128)S(1)} %fusion.24), channel_id=1, replica_groups=mesh['row'=4,'col'=8] {'row'}, use_global_device_ids=true, to_apply=%region_12.13 | all-reduce | flops 8192 | bytes 65536 | tf_op jit(solution)/shard_map/psum | solution.py:108
  188.1 46.0 %reduce-scatter.3.cloned.1.call-done = bf16[64,32]{0,1:T(8,128)(2,1)} async-done(((bf16[64,256]{0,1:T(8,128)(2,1)}), bf16[64,32]{0,1:T(8,128)(2,1)}) %reduce-scatter.3.cloned.1.call-update) | async-done | bytes 4112 | tf_op jit(solution)/shard_map/reduce_scatter | solution.py:105
  234.1 72.8 %all-reduce.12.cloned.1.call-done = (f32[64,128]{0,1:T(8,128)}, f32[64,128]{0,1:T(8,128)}) async-done(((f32[64,128]{0,1:T(8,128)}, f32[64,128]{0,1:T(8,128)}), (f32[64,128]{0,1:T(8,128)}, f32[64,128]{0,1:T(8,128)})) %all-reduce.12.cloned.1.call-update) | async-done | bytes 65552 | tf_op jit(solution)/shard_map/psum | solution.py:11
  308.4 0.8 collective-permute-start.7
  309.3 3.9 collective-permute-start.8
  313.2 1.6 collective-permute-done.7
  314.8 4.7 collective-permute-start.10
  319.6 1.6 collective-permute-done.9
  321.2 4.7 collective-permute-start.12
  325.9 1.7 collective-permute-done.11
  327.6 6.3 %collective-permute-done.13 = bf16[64,32]{0,1:T(8,128)(2,1)S(1)} collective-permute-done((bf16[64,32]{0,1:T(8,128)(2,1)S(1)}, bf16[64,32]{0,1:T(8,128)(2,1)S(1)}, u32[]{:S(2)}, u32[]{:S(2)}) %collective-permute-start.13) | collective-permute-done | bytes 4128 | tf_op jit(solution)/shard_map/ppermute | solution.py:87
  334.1 10.3 %psum.100 = bf16[64,128]{0,1:T(8,128)(2,1)S(1)} all-reduce(bf16[64,128]{0,1:T(8,128)(2,1)S(1)} %dynamic-slice_select_fusion.1), channel_id=1, replica_groups=mesh['row'=4,'col'=8] {'row'}, use_global_device_ids=true, to_apply=%region_15.16 | all-reduce | flops 8192 | bytes 32768 | tf_op jit(solution)/shard_map/psum | solution.py:11
  345.3 11.4 %psum.101 = f32[64,128]{0,1:T(8,128)S(1)} all-reduce(f32[64,128]{0,1:T(8,128)S(1)} %fusion.25), channel_id=1, replica_groups=mesh['row'=4,'col'=8] {'row'}, use_global_device_ids=true, to_apply=%region_17.18 | all-reduce | flops 8192 | bytes 65536 | tf_op jit(solution)/shard_map/psum | solution.py:108
  357.4 46.6 %reduce-scatter.5.cloned.1.call-done = bf16[64,32]{0,1:T(8,128)(2,1)} async-done(((bf16[64,256]{0,1:T(8,128)(2,1)}), bf16[64,32]{0,1:T(8,128)(2,1)}) %reduce-scatter.5.cloned.1.call-update) | async-done | bytes 4112 | tf_op jit(solution)/shard_map/reduce_scatter | solution.py:105
  404.0 72.3 %all-reduce.10.cloned.1.call-done = (f32[64,128]{0,1:T(8,128)}, f32[64,128]{0,1:T(8,128)}) async-done(((f32[64,128]{0,1:T(8,128)}, f32[64,128]{0,1:T(8,128)}), (f32[64,128]{0,1:T(8,128)}, f32[64,128]{0,1:T(8,128)})) %all-reduce.10.cloned.1.call-update) | async-done | bytes 65552 | tf_op jit(solution)/shard_map/psum | solution.py:11
  476.3 1.4 fusion.5
  (89 shorter events, 13.6 us)
Async XLA Ops:
  6.5 0.8 copy-start
  6.5 67.4 %all-reduce.8.cloned.1.call-start = ((), (), s32[]{:S(2)}) async-start(), calls=%async_computation.2 | async-start | bytes 393216 | tf_op jit(solution)/shard_map/psum | solution.py:11
  41.0 193.1 %reduce-scatter.3.cloned.1.call-start = ((), (), s32[]{:S(2)}) async-start(), calls=%async_computation.3 | async-start | bytes 73728 | tf_op jit(solution)/shard_map/reduce_scatter | solution.py:105
  41.2 0.7 copy-start.1
  42.5 0.7 copy-start.4
  44.3 0.7 copy-start.6
  46.2 0.7 copy-start.5
  139.1 0.7 copy-start.2
  139.9 6.3 %collective-permute-start = (bf16[64,32]{0,1:T(8,128)(2,1)S(1)}, bf16[64,32]{0,1:T(8,128)(2,1)S(1)}, u32[]{:S(2)}, u32[]{:S(2)}) collective-permute-start(bf16[64,32]{0,1:T(8,128)(2,1)S(1)} %get-tuple-element.16), channel_id=1, source_target_pairs={{0,1},{1,2},{2,3},{3,4},{4,5},{5,6},{6,7},{7,0},{8,9},{9,10},{10,1... | collective-permute-start | bytes 12296 | tf_op jit(solution)/shard_map/ppermute | solution.py:87
  139.9 6.3 %collective-permute-start.1 = (bf16[64,32]{0,1:T(8,128)(2,1)S(1)}, bf16[64,32]{0,1:T(8,128)(2,1)S(1)}, u32[]{:S(2)}, u32[]{:S(2)}) collective-permute-start(bf16[64,32]{0,1:T(8,128)(2,1)S(1)} %get-tuple-element.16), channel_id=1, source_target_pairs={{0,7},{1,0},{2,1},{3,2},{4,3},{5,4},{6,5},{7,6},{8,15},{9,8},{10,9... | collective-permute-start | bytes 12296 | tf_op jit(solution)/shard_map/ppermute | solution.py:92
  146.3 6.3 %collective-permute-start.2 = (bf16[64,32]{0,1:T(8,128)(2,1)S(1)}, bf16[64,32]{0,1:T(8,128)(2,1)S(1)}, u32[]{:S(2)}, u32[]{:S(2)}) collective-permute-start(bf16[64,32]{0,1:T(8,128)(2,1)S(1)} %collective-permute-done), channel_id=1, source_target_pairs={{0,1},{1,2},{2,3},{3,4},{4,5},{5,6},{6,7},{7,0},{8,9},{9,10},{10,1... | collective-permute-start | bytes 12296 | tf_op jit(solution)/shard_map/ppermute | solution.py:87
  146.3 6.3 %collective-permute-start.3 = (bf16[64,32]{0,1:T(8,128)(2,1)S(1)}, bf16[64,32]{0,1:T(8,128)(2,1)S(1)}, u32[]{:S(2)}, u32[]{:S(2)}) collective-permute-start(bf16[64,32]{0,1:T(8,128)(2,1)S(1)} %collective-permute-done.1), channel_id=1, source_target_pairs={{0,7},{1,0},{2,1},{3,2},{4,3},{5,4},{6,5},{7,6},{8,15},{9,8},{10,9... | collective-permute-start | bytes 12296 | tf_op jit(solution)/shard_map/ppermute | solution.py:92
  152.6 6.3 %collective-permute-start.4 = (bf16[64,32]{0,1:T(8,128)(2,1)S(1)}, bf16[64,32]{0,1:T(8,128)(2,1)S(1)}, u32[]{:S(2)}, u32[]{:S(2)}) collective-permute-start(bf16[64,32]{0,1:T(8,128)(2,1)S(1)} %collective-permute-done.2), channel_id=1, source_target_pairs={{0,1},{1,2},{2,3},{3,4},{4,5},{5,6},{6,7},{7,0},{8,9},{9,10},{10,1... | collective-permute-start | bytes 12296 | tf_op jit(solution)/shard_map/ppermute | solution.py:87
  152.6 6.4 %collective-permute-start.5 = (bf16[64,32]{0,1:T(8,128)(2,1)S(1)}, bf16[64,32]{0,1:T(8,128)(2,1)S(1)}, u32[]{:S(2)}, u32[]{:S(2)}) collective-permute-start(bf16[64,32]{0,1:T(8,128)(2,1)S(1)} %collective-permute-done.3), channel_id=1, source_target_pairs={{0,7},{1,0},{2,1},{3,2},{4,3},{5,4},{6,5},{7,6},{8,15},{9,8},{10,9... | collective-permute-start | bytes 12296 | tf_op jit(solution)/shard_map/ppermute | solution.py:92
  159.0 6.3 %collective-permute-start.6 = (bf16[64,32]{0,1:T(8,128)(2,1)S(1)}, bf16[64,32]{0,1:T(8,128)(2,1)S(1)}, u32[]{:S(2)}, u32[]{:S(2)}) collective-permute-start(bf16[64,32]{0,1:T(8,128)(2,1)S(1)} %collective-permute-done.4), channel_id=1, source_target_pairs={{0,1},{1,2},{2,3},{3,4},{4,5},{5,6},{6,7},{7,0},{8,9},{9,10},{10,1... | collective-permute-start | bytes 12296 | tf_op jit(solution)/shard_map/ppermute | solution.py:87
  176.6 130.3 %all-reduce.12.cloned.1.call-start = ((), (), s32[]{:S(2)}) async-start(), calls=%async_computation.6 | async-start | bytes 262144 | tf_op jit(solution)/shard_map/psum | solution.py:11
  188.1 215.9 %reduce-scatter.5.cloned.1.call-start = ((), (), s32[]{:S(2)}) async-start(), calls=%async_computation.4 | async-start | bytes 73728 | tf_op jit(solution)/shard_map/reduce_scatter | solution.py:105
  306.9 0.7 copy-start.3
  308.4 6.4 %collective-permute-start.7 = (bf16[64,32]{0,1:T(8,128)(2,1)S(1)}, bf16[64,32]{0,1:T(8,128)(2,1)S(1)}, u32[]{:S(2)}, u32[]{:S(2)}) collective-permute-start(bf16[64,32]{0,1:T(8,128)(2,1)S(1)} %get-tuple-element.12), channel_id=1, source_target_pairs={{0,1},{1,2},{2,3},{3,4},{4,5},{5,6},{6,7},{7,0},{8,9},{9,10},{10,1... | collective-permute-start | bytes 12296 | tf_op jit(solution)/shard_map/ppermute | solution.py:87
  309.3 5.6 %collective-permute-start.8 = (bf16[64,32]{0,1:T(8,128)(2,1)S(1)}, bf16[64,32]{0,1:T(8,128)(2,1)S(1)}, u32[]{:S(2)}, u32[]{:S(2)}) collective-permute-start(bf16[64,32]{0,1:T(8,128)(2,1)S(1)} %get-tuple-element.12), channel_id=1, source_target_pairs={{0,7},{1,0},{2,1},{3,2},{4,3},{5,4},{6,5},{7,6},{8,15},{9,8},{10,9... | collective-permute-start | bytes 12296 | tf_op jit(solution)/shard_map/ppermute | solution.py:92
  314.8 6.3 %collective-permute-start.9 = (bf16[64,32]{0,1:T(8,128)(2,1)S(1)}, bf16[64,32]{0,1:T(8,128)(2,1)S(1)}, u32[]{:S(2)}, u32[]{:S(2)}) collective-permute-start(bf16[64,32]{0,1:T(8,128)(2,1)S(1)} %collective-permute-done.7), channel_id=1, source_target_pairs={{0,1},{1,2},{2,3},{3,4},{4,5},{5,6},{6,7},{7,0},{8,9},{9,10},{10,1... | collective-permute-start | bytes 12296 | tf_op jit(solution)/shard_map/ppermute | solution.py:87
  314.8 6.3 %collective-permute-start.10 = (bf16[64,32]{0,1:T(8,128)(2,1)S(1)}, bf16[64,32]{0,1:T(8,128)(2,1)S(1)}, u32[]{:S(2)}, u32[]{:S(2)}) collective-permute-start(bf16[64,32]{0,1:T(8,128)(2,1)S(1)} %collective-permute-done.8), channel_id=1, source_target_pairs={{0,7},{1,0},{2,1},{3,2},{4,3},{5,4},{6,5},{7,6},{8,15},{9,8},{10,9... | collective-permute-start | bytes 12296 | tf_op jit(solution)/shard_map/ppermute | solution.py:92
  321.2 6.4 %collective-permute-start.11 = (bf16[64,32]{0,1:T(8,128)(2,1)S(1)}, bf16[64,32]{0,1:T(8,128)(2,1)S(1)}, u32[]{:S(2)}, u32[]{:S(2)}) collective-permute-start(bf16[64,32]{0,1:T(8,128)(2,1)S(1)} %collective-permute-done.9), channel_id=1, source_target_pairs={{0,1},{1,2},{2,3},{3,4},{4,5},{5,6},{6,7},{7,0},{8,9},{9,10},{10,1... | collective-permute-start | bytes 12296 | tf_op jit(solution)/shard_map/ppermute | solution.py:87
  321.2 6.4 %collective-permute-start.12 = (bf16[64,32]{0,1:T(8,128)(2,1)S(1)}, bf16[64,32]{0,1:T(8,128)(2,1)S(1)}, u32[]{:S(2)}, u32[]{:S(2)}) collective-permute-start(bf16[64,32]{0,1:T(8,128)(2,1)S(1)} %collective-permute-done.10), channel_id=1, source_target_pairs={{0,7},{1,0},{2,1},{3,2},{4,3},{5,4},{6,5},{7,6},{8,15},{9,8},{10,9... | collective-permute-start | bytes 12296 | tf_op jit(solution)/shard_map/ppermute | solution.py:92
  327.6 6.3 %collective-permute-start.13 = (bf16[64,32]{0,1:T(8,128)(2,1)S(1)}, bf16[64,32]{0,1:T(8,128)(2,1)S(1)}, u32[]{:S(2)}, u32[]{:S(2)}) collective-permute-start(bf16[64,32]{0,1:T(8,128)(2,1)S(1)} %collective-permute-done.11), channel_id=1, source_target_pairs={{0,1},{1,2},{2,3},{3,4},{4,5},{5,6},{6,7},{7,0},{8,9},{9,10},{10,1... | collective-permute-start | bytes 12296 | tf_op jit(solution)/shard_map/ppermute | solution.py:87
  345.2 131.0 %all-reduce.10.cloned.1.call-start = ((), (), s32[]{:S(2)}) async-start(), calls=%async_computation.5 | async-start | bytes 262144 | tf_op jit(solution)/shard_map/psum | solution.py:11
Sparse Core Ops, SparseCore 0:
  41.1 32.7 all-reduce.7
  176.7 57.3 reduce-scatter.2
  238.0 68.8 all-reduce.11
  345.4 58.6 reduce-scatter.4
  407.3 68.8 all-reduce.9
